TPU v7x, 256 devices: a whole 4x4x8 slice. The times are simulated.
256 devices in a mesh: seq: 64 (over z_hi, y, x, core), tp: 4 (over z_lo).
Axes of the slice: x: 4, y: 4, z: 8 (z_hi: 2, z_lo: 4; z = z_hi * 4 + z_lo), core: 2. Of those that a mesh axis runs over, the one named last changes fastest.
Arguments:
- residual: bfloat16 [32768, 2048], P('seq', 'tp'), may hold values from -6 to 6
- norm_gain: float32 [2048], replicated, may hold values from 0.3 to 3
- query_weight: bfloat16 [2048, 1024], P(None, 'tp'), as said below
- key_weight: bfloat16 [2048, 1024], P(None, 'tp'), as said below
- value_weight: bfloat16 [2048, 1024], P(None, 'tp'), may hold values from -0.375 to 0.375
- out_weight: bfloat16 [1024, 2048], P('tp'), may hold values from -0.1875 to 0.1875
- segment_start: int32 [32768], P('seq'), may hold values from 0 to 32640, as said below
- token_valid: int32 [32768], P('seq'), may hold values from 0 to 1, as said below
- page_slot: int32 [256], P('seq'), may hold values from 4 to 511, as said below
Outputs:
- hidden: bfloat16 [32768, 2048], P('seq', 'tp')
- cache: bfloat16 [512, 128, 2048], P('seq', None, 'tp')
Inputs may be any that keep to these rules, and one draw needn't show every extreme that they name: `segment_start`: prompts start at multiples of 128 and are contiguous; each holds at most 8192 tokens and one holds exactly 8192. `token_valid`: zeros form a tail of the last page of a prompt; the first token of every prompt is 1. No two pages share a cache page; page_slot // 8 is the device that holds the page's tokens, or the next device when that one holds tokens of the same prompt. `query_weight`: independent entries whose scale falls as the inverse square root of 2048. `key_weight`: independent entries whose scale falls as the inverse square root of 2048.
All inputs are finite; a program needn't handle non-finite values.
Results may differ from a plain program's by a relative error of at most 0.02.
The roundings to bfloat16 on the way count: a program that leaves them out, or rounds other values in their place, can miss the bound.
Values may be sent and summed in bfloat16 or wider, within the bound.
No kernel may reach another device: no remote copies, remote signals or barrier semaphores. Data moves between devices by JAX's collectives and lax.ppermute only.
A program may use at most 128 MiB of HBM per device.

v0:
```python
import jax
import jax.numpy as jnp
from jax import lax
from jax.sharding import PartitionSpec as P

HD = 64
PAGE = 128
SPAN = 16
THETA = 130000.0
EPS = 1e-05


def passed_along(x, axis, by):
    count = lax.axis_size(axis)
    pairs = [(i, i + by) for i in range(count) if 0 <= i + by < count]
    return lax.ppermute(x, axis, pairs)


def rotate(inputs, positions):
    half_dim = inputs.shape[-1] // 2
    frequency = THETA ** (-2.0 * jnp.arange(half_dim, dtype=jnp.float32) / inputs.shape[-1])
    angles = positions.astype(jnp.float32)[:, None] * frequency[None, :]
    cosine = jnp.cos(angles)[:, None, :]
    sine_part = jnp.sin(angles)[:, None, :]
    front_half = inputs[..., :half_dim]
    back_half = inputs[..., half_dim:]
    return jnp.concatenate(
        [front_half * cosine - back_half * sine_part, back_half * cosine + front_half * sine_part],
        axis=-1,
    )


def body(
    residual,
    norm_gain,
    query_weight,
    key_weight,
    value_weight,
    out_weight,
    segment_start,
    token_valid,
    page_slot,
):
    row_count = residual.shape[0]
    local_heads = query_weight.shape[1] // HD
    gathered = lax.all_gather(residual, "tp", axis=1, tiled=True)
    widened = gathered.astype(jnp.float32)
    mean_sq = jnp.mean(widened * widened, axis=1, keepdims=True)
    normed = (widened * lax.rsqrt(mean_sq + EPS) * norm_gain[None, :]).astype(jnp.bfloat16)
    seq_rank = lax.axis_index("seq")
    first_row = seq_rank * row_count
    places = first_row + jnp.arange(row_count, dtype=jnp.int32)
    offsets = places - segment_start
    queries = jnp.dot(normed, query_weight, preferred_element_type=jnp.float32).reshape(
        row_count, local_heads, HD
    )
    queries = rotate(queries, offsets).astype(jnp.bfloat16)
    key_rot = jnp.dot(normed, key_weight, preferred_element_type=jnp.float32).reshape(
        row_count, local_heads, HD
    )
    key_rot = rotate(key_rot, offsets).astype(jnp.bfloat16)
    values = (
        jnp.dot(normed, value_weight, preferred_element_type=jnp.float32)
        .reshape(row_count, local_heads, HD)
        .astype(jnp.bfloat16)
    )
    packed = jnp.concatenate([key_rot[:, :, None, :], values[:, :, None, :]], axis=2).reshape(
        row_count, local_heads * 2 * HD
    )
    packed = jnp.where(token_valid[:, None] > 0, packed, jnp.zeros_like(packed))
    key_group = jnp.where(token_valid > 0, segment_start, -1)
    in_page = jnp.arange(row_count, dtype=jnp.int32) % PAGE
    page_rows = jnp.repeat(page_slot, PAGE) * PAGE + in_page
    slot_count = 2 * page_slot.shape[0]
    cache_size = slot_count * PAGE
    base_row = seq_rank * cache_size
    score_scale = HD ** (-0.5)

    def attend_block(running, incoming, allowed):
        row_max, norm_sum, weighted = running
        key_value = incoming[0].reshape(incoming[0].shape[0], local_heads, 2, HD)
        scores = (
            jnp.einsum(
                "qhd,khd->hqk", queries, key_value[:, :, 0, :], preferred_element_type=jnp.float32
            )
            * score_scale
        )
        block_max = jnp.max(jnp.where(allowed[None], scores, -1e30), axis=2)
        new_max = jnp.maximum(row_max, block_max)
        weights = jnp.where(allowed[None], jnp.exp(scores - new_max[:, :, None]), 0.0)
        shrink = jnp.exp(row_max - new_max)
        norm_sum = norm_sum * shrink + jnp.sum(weights, axis=2)
        update = jnp.einsum(
            "hqk,khd->qhd",
            weights.astype(jnp.bfloat16),
            key_value[:, :, 1, :],
            preferred_element_type=jnp.float32,
        )
        weighted = weighted * jnp.transpose(shrink)[:, :, None] + update
        return (new_max, norm_sum, weighted)

    def absorb(carried, incoming, begin_row):
        row_max, norm_sum, weighted, cache_rows = carried
        key_count = incoming[0].shape[0]
        key_places = begin_row + jnp.arange(key_count, dtype=jnp.int32)
        allowed = (
            (incoming[1][None, :] == segment_start[:, None])
            & (key_places[None, :] <= places[:, None])
            & (key_places[None, :] >= 0)
        )
        local_dest = incoming[2] - base_row
        in_range = (local_dest >= 0) & (local_dest < cache_size) & (key_places >= 0)
        target = jnp.where(in_range, local_dest, cache_size)
        cache_rows = cache_rows.at[target].set(incoming[0], mode="drop")
        running = attend_block((row_max, norm_sum, weighted), incoming, allowed)
        return (running[0], running[1], running[2], cache_rows)

    initial = (
        jnp.full((local_heads, row_count), -1e30, jnp.float32),
        jnp.zeros((local_heads, row_count), jnp.float32),
        jnp.zeros((row_count, local_heads, HD), jnp.float32),
        jnp.zeros((cache_size, local_heads * 2 * HD), jnp.bfloat16),
    )
    own_block = (packed, key_group, page_rows)
    carried = absorb(initial, own_block, first_row)
    reach_dev = min(SPAN, lax.axis_size("seq") // 2)

    def advance(step_index, carry_in):
        moving, carry_state = carry_in
        moving = passed_along((moving[0], moving[1], moving[2]), "seq", 1)
        carry_state = absorb(carry_state, moving, first_row - (step_index + 1) * row_count)
        return (moving, carry_state)

    moving, carried = lax.fori_loop(0, reach_dev, advance, (own_block, carried))
    row_max, norm_sum, weighted, cache_rows = carried
    attended = (
        (weighted / jnp.transpose(norm_sum)[:, :, None])
        .astype(jnp.bfloat16)
        .reshape(row_count, local_heads * HD)
    )
    projected = jnp.dot(attended, out_weight, preferred_element_type=jnp.float32)
    summed = lax.psum_scatter(
        projected.astype(jnp.bfloat16), "tp", scatter_dimension=1, tiled=True
    ).astype(jnp.float32)
    hidden = (residual.astype(jnp.float32) + summed).astype(jnp.bfloat16)
    return (hidden, cache_rows.reshape(slot_count, PAGE, local_heads * 2 * HD))


def solution(mesh):
    return jax.shard_map(
        body,
        mesh=mesh,
        in_specs=(
            P("seq", "tp"),
            P(),
            P(None, "tp"),
            P(None, "tp"),
            P(None, "tp"),
            P("tp", None),
            P("seq"),
            P("seq"),
            P("seq"),
        ),
        out_specs=(P("seq", "tp"), P("seq", None, "tp")),
        check_vma=False,
    )
```

profile of v0, /device:TPU:1, one launch (start us, length us, event | category | flops | bytes accessed | tf_op | source)
XLA Modules:
  0.0 631.6 jit_solution(17440001359176810723)
XLA Ops:
  10.9 52.2 %all-gather.2.cloned.1.call-done = bf16[512,2048]{1,0:T(8,128)(2,1)} async-done(((bf16[512,512]{1,0:T(8,128)(2,1)}), bf16[512,2048]{1,0:T(8,128)(2,1)}) %all-gather.2.cloned.1.call-update) | async-done | bytes 2097168 | tf_op jit(solution)/shard_map/all_gather | solution.py:46
  77.5 398.4 %while.27 = (s32[]{:T(128)}, bf16[512,512]{0,1:T(8,128)(2,1)S(1)}, s32[512]{0:T(512)S(1)}, s32[512]{0:T(512)S(1)}, f32[4,512]{1,0:T(4,128)S(1)}, /*index=5*/f32[...) while((s32[]{:T(128)}, bf16[512,512]{0,1:T(8,128)(2,1)S(1)}, ...), condition=%wide.region_8.9_spmd.clone.clone, body=%wide.region_4.8_spmd.clone.clone.sunk | while | flops 281293824 | bytes 21409060 | solution.py:134
  77.5 4.2 collective-permute-start.2
  87.5 5.7 collective-permute-done
  101.2 4.4 collective-permute-start.2
  111.2 5.7 collective-permute-done
  124.9 4.4 collective-permute-start.2
  135.1 5.7 collective-permute-done
  148.8 4.4 collective-permute-start.2
  156.4 4.4 collective-permute-start
  161.2 5.7 collective-permute-done
  174.9 4.4 collective-permute-start.2
  181.2 4.0 collective-permute-start
  185.7 5.7 collective-permute-done
  199.4 4.4 collective-permute-start.2
  205.7 4.0 collective-permute-start
  210.1 5.7 collective-permute-done
  223.9 4.4 collective-permute-start.2
  230.2 4.0 collective-permute-start
  234.6 5.7 collective-permute-done
  248.4 4.4 collective-permute-start.2
  254.7 4.0 collective-permute-start
  259.1 5.7 collective-permute-done
  272.8 4.4 collective-permute-start.2
  279.2 4.0 collective-permute-start
  283.6 5.7 collective-permute-done
  297.3 4.4 collective-permute-start.2
  303.7 4.0 collective-permute-start
  308.1 5.7 collective-permute-done
  321.8 4.4 collective-permute-start.2
  328.1 4.0 collective-permute-start
  332.6 5.7 collective-permute-done
  346.3 4.4 collective-permute-start.2
  352.6 4.0 collective-permute-start
  357.1 5.7 collective-permute-done
  370.8 4.4 collective-permute-start.2
  377.1 4.0 collective-permute-start
  381.6 5.7 collective-permute-done
  395.3 4.4 collective-permute-start.2
  401.6 4.0 collective-permute-start
  406.1 5.7 collective-permute-done
  419.8 4.4 collective-permute-start.2
  430.5 5.7 collective-permute-done
  444.3 4.4 collective-permute-start.2
  448.7 8.7 %collective-permute-start.1 = (s32[512]{0:T(512)S(1)}, s32[512]{0:T(512)S(1)}, u32[]{:S(2)}, u32[]{:S(2)}) collective-permute-start(s32[512]{0:T(512)S(1)} %get-tuple-element.427), channel_id=1, source_target_pairs={{0,4},{4,8},{8,12},{12,16},{16,20},{20,24},{24,28},{28,32},{32,36}... | collective-permute-start | bytes 6152 | tf_op jit(solution)/shard_map/while/body/eval_jaxpr/ppermute | solution.py:16
  457.4 4.4 collective-permute-start
  462.2 5.7 collective-permute-done
  479.5 143.3 %reduce-scatter.2.cloned.1.call-done = bf16[512,512]{1,0:T(8,128)(2,1)} async-done(((bf16[512,2048]{1,0:T(8,128)(2,1)}), bf16[512,512]{1,0:T(8,128)(2,1)}) %reduce-scatter.2.cloned.1.call-update) | async-done | bytes 524304 | tf_op jit(solution)/shard_map/reduce_scatter | solution.py:142
  (340 shorter events, 200.5 us)
Async XLA Ops:
  7.2 55.9 %all-gather.2.cloned.1.call-start = ((), (), s32[]{:S(2)}) async-start(), calls=%async_computation.1 | async-start | bytes 2621440 | tf_op jit(solution)/shard_map/all_gather | solution.py:46
  7.9 614.9 %reduce-scatter.2.cloned.1.call-start = ((), (), s32[]{:S(2)}) async-start(), calls=%async_computation.2 | async-start | bytes 2621440 | tf_op jit(solution)/shard_map/reduce_scatter | solution.py:142
  77.5 9.6 %collective-permute-start.2 = (s32[512]{0:T(512)S(1)}, s32[512]{0:T(512)S(1)}, u32[]{:S(2)}, u32[]{:S(2)}) collective-permute-start(s32[512]{0:T(512)S(1)} %get-tuple-element.428), channel_id=1, source_target_pairs={{0,4},{4,8},{8,12},{12,16},{16,20},{20,24},{24,28},{28,32},{32,36}... | collective-permute-start | bytes 6152 | tf_op jit(solution)/shard_map/while/body/eval_jaxpr/ppermute | solution.py:16
  83.6 9.6 %collective-permute-start = (bf16[512,512]{0,1:T(8,128)(2,1)S(1)}, bf16[512,512]{0,1:T(8,128)(2,1)S(1)}, u32[]{:S(2)}, u32[]{:S(2)}) collective-permute-start(bf16[512,512]{0,1:T(8,128)(2,1)S(1)} %get-tuple-element.426), channel_id=1, source_target_pairs={{0,4},{4,8},{8,12},{12,16},{16,20},{20,24},{24,28},{28,32},{32,36}... | collective-permute-start | bytes 1572872 | tf_op jit(solution)/shard_map/while/body/eval_jaxpr/ppermute | solution.py:16
  101.2 9.6 %collective-permute-start.2 = (s32[512]{0:T(512)S(1)}, s32[512]{0:T(512)S(1)}, u32[]{:S(2)}, u32[]{:S(2)}) collective-permute-start(s32[512]{0:T(512)S(1)} %get-tuple-element.428), channel_id=1, source_target_pairs={{0,4},{4,8},{8,12},{12,16},{16,20},{20,24},{24,28},{28,32},{32,36}... | collective-permute-start | bytes 6152 | tf_op jit(solution)/shard_map/while/body/eval_jaxpr/ppermute | solution.py:16
  107.6 9.3 %collective-permute-start = (bf16[512,512]{0,1:T(8,128)(2,1)S(1)}, bf16[512,512]{0,1:T(8,128)(2,1)S(1)}, u32[]{:S(2)}, u32[]{:S(2)}) collective-permute-start(bf16[512,512]{0,1:T(8,128)(2,1)S(1)} %get-tuple-element.426), channel_id=1, source_target_pairs={{0,4},{4,8},{8,12},{12,16},{16,20},{20,24},{24,28},{28,32},{32,36}... | collective-permute-start | bytes 1572872 | tf_op jit(solution)/shard_map/while/body/eval_jaxpr/ppermute | solution.py:16
  124.9 9.9 %collective-permute-start.2 = (s32[512]{0:T(512)S(1)}, s32[512]{0:T(512)S(1)}, u32[]{:S(2)}, u32[]{:S(2)}) collective-permute-start(s32[512]{0:T(512)S(1)} %get-tuple-element.428), channel_id=1, source_target_pairs={{0,4},{4,8},{8,12},{12,16},{16,20},{20,24},{24,28},{28,32},{32,36}... | collective-permute-start | bytes 6152 | tf_op jit(solution)/shard_map/while/body/eval_jaxpr/ppermute | solution.py:16
  129.3 5.4 collective-permute-start.1
  131.2 9.6 %collective-permute-start = (bf16[512,512]{0,1:T(8,128)(2,1)S(1)}, bf16[512,512]{0,1:T(8,128)(2,1)S(1)}, u32[]{:S(2)}, u32[]{:S(2)}) collective-permute-start(bf16[512,512]{0,1:T(8,128)(2,1)S(1)} %get-tuple-element.426), channel_id=1, source_target_pairs={{0,4},{4,8},{8,12},{12,16},{16,20},{20,24},{24,28},{28,32},{32,36}... | collective-permute-start | bytes 1572872 | tf_op jit(solution)/shard_map/while/body/eval_jaxpr/ppermute | solution.py:16
  148.8 12.0 %collective-permute-start.2 = (s32[512]{0:T(512)S(1)}, s32[512]{0:T(512)S(1)}, u32[]{:S(2)}, u32[]{:S(2)}) collective-permute-start(s32[512]{0:T(512)S(1)} %get-tuple-element.428), channel_id=1, source_target_pairs={{0,4},{4,8},{8,12},{12,16},{16,20},{20,24},{24,28},{28,32},{32,36}... | collective-permute-start | bytes 6152 | tf_op jit(solution)/shard_map/while/body/eval_jaxpr/ppermute | solution.py:16
  153.2 7.6 %collective-permute-start.1 = (s32[512]{0:T(512)S(1)}, s32[512]{0:T(512)S(1)}, u32[]{:S(2)}, u32[]{:S(2)}) collective-permute-start(s32[512]{0:T(512)S(1)} %get-tuple-element.427), channel_id=1, source_target_pairs={{0,4},{4,8},{8,12},{12,16},{16,20},{20,24},{24,28},{28,32},{32,36}... | collective-permute-start | bytes 6152 | tf_op jit(solution)/shard_map/while/body/eval_jaxpr/ppermute | solution.py:16
  156.4 10.5 %collective-permute-start = (bf16[512,512]{0,1:T(8,128)(2,1)S(1)}, bf16[512,512]{0,1:T(8,128)(2,1)S(1)}, u32[]{:S(2)}, u32[]{:S(2)}) collective-permute-start(bf16[512,512]{0,1:T(8,128)(2,1)S(1)} %get-tuple-element.426), channel_id=1, source_target_pairs={{0,4},{4,8},{8,12},{12,16},{16,20},{20,24},{24,28},{28,32},{32,36}... | collective-permute-start | bytes 1572872 | tf_op jit(solution)/shard_map/while/body/eval_jaxpr/ppermute | solution.py:16
  174.9 10.4 %collective-permute-start.2 = (s32[512]{0:T(512)S(1)}, s32[512]{0:T(512)S(1)}, u32[]{:S(2)}, u32[]{:S(2)}) collective-permute-start(s32[512]{0:T(512)S(1)} %get-tuple-element.428), channel_id=1, source_target_pairs={{0,4},{4,8},{8,12},{12,16},{16,20},{20,24},{24,28},{28,32},{32,36}... | collective-permute-start | bytes 6152 | tf_op jit(solution)/shard_map/while/body/eval_jaxpr/ppermute | solution.py:16
  179.3 6.0 collective-permute-start.1
  181.2 10.1 %collective-permute-start = (bf16[512,512]{0,1:T(8,128)(2,1)S(1)}, bf16[512,512]{0,1:T(8,128)(2,1)S(1)}, u32[]{:S(2)}, u32[]{:S(2)}) collective-permute-start(bf16[512,512]{0,1:T(8,128)(2,1)S(1)} %get-tuple-element.426), channel_id=1, source_target_pairs={{0,4},{4,8},{8,12},{12,16},{16,20},{20,24},{24,28},{28,32},{32,36}... | collective-permute-start | bytes 1572872 | tf_op jit(solution)/shard_map/while/body/eval_jaxpr/ppermute | solution.py:16
  199.4 10.4 %collective-permute-start.2 = (s32[512]{0:T(512)S(1)}, s32[512]{0:T(512)S(1)}, u32[]{:S(2)}, u32[]{:S(2)}) collective-permute-start(s32[512]{0:T(512)S(1)} %get-tuple-element.428), channel_id=1, source_target_pairs={{0,4},{4,8},{8,12},{12,16},{16,20},{20,24},{24,28},{28,32},{32,36}... | collective-permute-start | bytes 6152 | tf_op jit(solution)/shard_map/while/body/eval_jaxpr/ppermute | solution.py:16
  203.8 6.0 collective-permute-start.1
  205.7 10.1 %collective-permute-start = (bf16[512,512]{0,1:T(8,128)(2,1)S(1)}, bf16[512,512]{0,1:T(8,128)(2,1)S(1)}, u32[]{:S(2)}, u32[]{:S(2)}) collective-permute-start(bf16[512,512]{0,1:T(8,128)(2,1)S(1)} %get-tuple-element.426), channel_id=1, source_target_pairs={{0,4},{4,8},{8,12},{12,16},{16,20},{20,24},{24,28},{28,32},{32,36}... | collective-permute-start | bytes 1572872 | tf_op jit(solution)/shard_map/while/body/eval_jaxpr/ppermute | solution.py:16
  223.9 10.4 %collective-permute-start.2 = (s32[512]{0:T(512)S(1)}, s32[512]{0:T(512)S(1)}, u32[]{:S(2)}, u32[]{:S(2)}) collective-permute-start(s32[512]{0:T(512)S(1)} %get-tuple-element.428), channel_id=1, source_target_pairs={{0,4},{4,8},{8,12},{12,16},{16,20},{20,24},{24,28},{28,32},{32,36}... | collective-permute-start | bytes 6152 | tf_op jit(solution)/shard_map/while/body/eval_jaxpr/ppermute | solution.py:16
  228.3 6.0 collective-permute-start.1
  230.2 10.1 %collective-permute-start = (bf16[512,512]{0,1:T(8,128)(2,1)S(1)}, bf16[512,512]{0,1:T(8,128)(2,1)S(1)}, u32[]{:S(2)}, u32[]{:S(2)}) collective-permute-start(bf16[512,512]{0,1:T(8,128)(2,1)S(1)} %get-tuple-element.426), channel_id=1, source_target_pairs={{0,4},{4,8},{8,12},{12,16},{16,20},{20,24},{24,28},{28,32},{32,36}... | collective-permute-start | bytes 1572872 | tf_op jit(solution)/shard_map/while/body/eval_jaxpr/ppermute | solution.py:16
  248.4 10.4 %collective-permute-start.2 = (s32[512]{0:T(512)S(1)}, s32[512]{0:T(512)S(1)}, u32[]{:S(2)}, u32[]{:S(2)}) collective-permute-start(s32[512]{0:T(512)S(1)} %get-tuple-element.428), channel_id=1, source_target_pairs={{0,4},{4,8},{8,12},{12,16},{16,20},{20,24},{24,28},{28,32},{32,36}... | collective-permute-start | bytes 6152 | tf_op jit(solution)/shard_map/while/body/eval_jaxpr/ppermute | solution.py:16
  252.7 6.0 collective-permute-start.1
  254.7 10.1 %collective-permute-start = (bf16[512,512]{0,1:T(8,128)(2,1)S(1)}, bf16[512,512]{0,1:T(8,128)(2,1)S(1)}, u32[]{:S(2)}, u32[]{:S(2)}) collective-permute-start(bf16[512,512]{0,1:T(8,128)(2,1)S(1)} %get-tuple-element.426), channel_id=1, source_target_pairs={{0,4},{4,8},{8,12},{12,16},{16,20},{20,24},{24,28},{28,32},{32,36}... | collective-permute-start | bytes 1572872 | tf_op jit(solution)/shard_map/while/body/eval_jaxpr/ppermute | solution.py:16
  272.8 10.4 %collective-permute-start.2 = (s32[512]{0:T(512)S(1)}, s32[512]{0:T(512)S(1)}, u32[]{:S(2)}, u32[]{:S(2)}) collective-permute-start(s32[512]{0:T(512)S(1)} %get-tuple-element.428), channel_id=1, source_target_pairs={{0,4},{4,8},{8,12},{12,16},{16,20},{20,24},{24,28},{28,32},{32,36}... | collective-permute-start | bytes 6152 | tf_op jit(solution)/shard_map/while/body/eval_jaxpr/ppermute | solution.py:16
  277.2 6.0 collective-permute-start.1
  279.2 10.1 %collective-permute-start = (bf16[512,512]{0,1:T(8,128)(2,1)S(1)}, bf16[512,512]{0,1:T(8,128)(2,1)S(1)}, u32[]{:S(2)}, u32[]{:S(2)}) collective-permute-start(bf16[512,512]{0,1:T(8,128)(2,1)S(1)} %get-tuple-element.426), channel_id=1, source_target_pairs={{0,4},{4,8},{8,12},{12,16},{16,20},{20,24},{24,28},{28,32},{32,36}... | collective-permute-start | bytes 1572872 | tf_op jit(solution)/shard_map/while/body/eval_jaxpr/ppermute | solution.py:16
  297.3 10.4 %collective-permute-start.2 = (s32[512]{0:T(512)S(1)}, s32[512]{0:T(512)S(1)}, u32[]{:S(2)}, u32[]{:S(2)}) collective-permute-start(s32[512]{0:T(512)S(1)} %get-tuple-element.428), channel_id=1, source_target_pairs={{0,4},{4,8},{8,12},{12,16},{16,20},{20,24},{24,28},{28,32},{32,36}... | collective-permute-start | bytes 6152 | tf_op jit(solution)/shard_map/while/body/eval_jaxpr/ppermute | solution.py:16
  301.7 6.0 collective-permute-start.1
  303.7 10.1 %collective-permute-start = (bf16[512,512]{0,1:T(8,128)(2,1)S(1)}, bf16[512,512]{0,1:T(8,128)(2,1)S(1)}, u32[]{:S(2)}, u32[]{:S(2)}) collective-permute-start(bf16[512,512]{0,1:T(8,128)(2,1)S(1)} %get-tuple-element.426), channel_id=1, source_target_pairs={{0,4},{4,8},{8,12},{12,16},{16,20},{20,24},{24,28},{28,32},{32,36}... | collective-permute-start | bytes 1572872 | tf_op jit(solution)/shard_map/while/body/eval_jaxpr/ppermute | solution.py:16
  321.8 10.4 %collective-permute-start.2 = (s32[512]{0:T(512)S(1)}, s32[512]{0:T(512)S(1)}, u32[]{:S(2)}, u32[]{:S(2)}) collective-permute-start(s32[512]{0:T(512)S(1)} %get-tuple-element.428), channel_id=1, source_target_pairs={{0,4},{4,8},{8,12},{12,16},{16,20},{20,24},{24,28},{28,32},{32,36}... | collective-permute-start | bytes 6152 | tf_op jit(solution)/shard_map/while/body/eval_jaxpr/ppermute | solution.py:16
  326.2 6.0 collective-permute-start.1
  328.1 10.1 %collective-permute-start = (bf16[512,512]{0,1:T(8,128)(2,1)S(1)}, bf16[512,512]{0,1:T(8,128)(2,1)S(1)}, u32[]{:S(2)}, u32[]{:S(2)}) collective-permute-start(bf16[512,512]{0,1:T(8,128)(2,1)S(1)} %get-tuple-element.426), channel_id=1, source_target_pairs={{0,4},{4,8},{8,12},{12,16},{16,20},{20,24},{24,28},{28,32},{32,36}... | collective-permute-start | bytes 1572872 | tf_op jit(solution)/shard_map/while/body/eval_jaxpr/ppermute | solution.py:16
  346.3 10.4 %collective-permute-start.2 = (s32[512]{0:T(512)S(1)}, s32[512]{0:T(512)S(1)}, u32[]{:S(2)}, u32[]{:S(2)}) collective-permute-start(s32[512]{0:T(512)S(1)} %get-tuple-element.428), channel_id=1, source_target_pairs={{0,4},{4,8},{8,12},{12,16},{16,20},{20,24},{24,28},{28,32},{32,36}... | collective-permute-start | bytes 6152 | tf_op jit(solution)/shard_map/while/body/eval_jaxpr/ppermute | solution.py:16
  350.7 6.0 collective-permute-start.1
  352.6 10.1 %collective-permute-start = (bf16[512,512]{0,1:T(8,128)(2,1)S(1)}, bf16[512,512]{0,1:T(8,128)(2,1)S(1)}, u32[]{:S(2)}, u32[]{:S(2)}) collective-permute-start(bf16[512,512]{0,1:T(8,128)(2,1)S(1)} %get-tuple-element.426), channel_id=1, source_target_pairs={{0,4},{4,8},{8,12},{12,16},{16,20},{20,24},{24,28},{28,32},{32,36}... | collective-permute-start | bytes 1572872 | tf_op jit(solution)/shard_map/while/body/eval_jaxpr/ppermute | solution.py:16
  370.8 10.4 %collective-permute-start.2 = (s32[512]{0:T(512)S(1)}, s32[512]{0:T(512)S(1)}, u32[]{:S(2)}, u32[]{:S(2)}) collective-permute-start(s32[512]{0:T(512)S(1)} %get-tuple-element.428), channel_id=1, source_target_pairs={{0,4},{4,8},{8,12},{12,16},{16,20},{20,24},{24,28},{28,32},{32,36}... | collective-permute-start | bytes 6152 | tf_op jit(solution)/shard_map/while/body/eval_jaxpr/ppermute | solution.py:16
  375.2 6.0 collective-permute-start.1
  377.1 10.1 %collective-permute-start = (bf16[512,512]{0,1:T(8,128)(2,1)S(1)}, bf16[512,512]{0,1:T(8,128)(2,1)S(1)}, u32[]{:S(2)}, u32[]{:S(2)}) collective-permute-start(bf16[512,512]{0,1:T(8,128)(2,1)S(1)} %get-tuple-element.426), channel_id=1, source_target_pairs={{0,4},{4,8},{8,12},{12,16},{16,20},{20,24},{24,28},{28,32},{32,36}... | collective-permute-start | bytes 1572872 | tf_op jit(solution)/shard_map/while/body/eval_jaxpr/ppermute | solution.py:16
  395.3 10.4 %collective-permute-start.2 = (s32[512]{0:T(512)S(1)}, s32[512]{0:T(512)S(1)}, u32[]{:S(2)}, u32[]{:S(2)}) collective-permute-start(s32[512]{0:T(512)S(1)} %get-tuple-element.428), channel_id=1, source_target_pairs={{0,4},{4,8},{8,12},{12,16},{16,20},{20,24},{24,28},{28,32},{32,36}... | collective-permute-start | bytes 6152 | tf_op jit(solution)/shard_map/while/body/eval_jaxpr/ppermute | solution.py:16
  399.7 6.0 collective-permute-start.1
  401.6 10.1 %collective-permute-start = (bf16[512,512]{0,1:T(8,128)(2,1)S(1)}, bf16[512,512]{0,1:T(8,128)(2,1)S(1)}, u32[]{:S(2)}, u32[]{:S(2)}) collective-permute-start(bf16[512,512]{0,1:T(8,128)(2,1)S(1)} %get-tuple-element.426), channel_id=1, source_target_pairs={{0,4},{4,8},{8,12},{12,16},{16,20},{20,24},{24,28},{28,32},{32,36}... | collective-permute-start | bytes 1572872 | tf_op jit(solution)/shard_map/while/body/eval_jaxpr/ppermute | solution.py:16
  419.8 10.4 %collective-permute-start.2 = (s32[512]{0:T(512)S(1)}, s32[512]{0:T(512)S(1)}, u32[]{:S(2)}, u32[]{:S(2)}) collective-permute-start(s32[512]{0:T(512)S(1)} %get-tuple-element.428), channel_id=1, source_target_pairs={{0,4},{4,8},{8,12},{12,16},{16,20},{20,24},{24,28},{28,32},{32,36}... | collective-permute-start | bytes 6152 | tf_op jit(solution)/shard_map/while/body/eval_jaxpr/ppermute | solution.py:16
  424.2 6.0 collective-permute-start.1
  426.1 10.1 %collective-permute-start = (bf16[512,512]{0,1:T(8,128)(2,1)S(1)}, bf16[512,512]{0,1:T(8,128)(2,1)S(1)}, u32[]{:S(2)}, u32[]{:S(2)}) collective-permute-start(bf16[512,512]{0,1:T(8,128)(2,1)S(1)} %get-tuple-element.426), channel_id=1, source_target_pairs={{0,4},{4,8},{8,12},{12,16},{16,20},{20,24},{24,28},{28,32},{32,36}... | collective-permute-start | bytes 1572872 | tf_op jit(solution)/shard_map/while/body/eval_jaxpr/ppermute | solution.py:16
  444.3 17.6 %collective-permute-start.2 = (s32[512]{0:T(512)S(1)}, s32[512]{0:T(512)S(1)}, u32[]{:S(2)}, u32[]{:S(2)}) collective-permute-start(s32[512]{0:T(512)S(1)} %get-tuple-element.428), channel_id=1, source_target_pairs={{0,4},{4,8},{8,12},{12,16},{16,20},{20,24},{24,28},{28,32},{32,36}... | collective-permute-start | bytes 6152 | tf_op jit(solution)/shard_map/while/body/eval_jaxpr/ppermute | solution.py:16
  448.7 13.2 %collective-permute-start.1 = (s32[512]{0:T(512)S(1)}, s32[512]{0:T(512)S(1)}, u32[]{:S(2)}, u32[]{:S(2)}) collective-permute-start(s32[512]{0:T(512)S(1)} %get-tuple-element.427), channel_id=1, source_target_pairs={{0,4},{4,8},{8,12},{12,16},{16,20},{20,24},{24,28},{28,32},{32,36}... | collective-permute-start | bytes 6152 | tf_op jit(solution)/shard_map/while/body/eval_jaxpr/ppermute | solution.py:16
  457.4 10.5 %collective-permute-start = (bf16[512,512]{0,1:T(8,128)(2,1)S(1)}, bf16[512,512]{0,1:T(8,128)(2,1)S(1)}, u32[]{:S(2)}, u32[]{:S(2)}) collective-permute-start(bf16[512,512]{0,1:T(8,128)(2,1)S(1)} %get-tuple-element.426), channel_id=1, source_target_pairs={{0,4},{4,8},{8,12},{12,16},{16,20},{20,24},{24,28},{28,32},{32,36}... | collective-permute-start | bytes 1572872 | tf_op jit(solution)/shard_map/while/body/eval_jaxpr/ppermute | solution.py:16
  (10 other events, 910.0 us)
Sparse Core Ops, SparseCore 0:
  9.8 53.2 all-gather.1
  479.7 143.1 reduce-scatter.1
where the time goes:
time: 634 us; the launch traced here: 632 us
  waiting for transfers between devices  287 us (45%)
  starting transfers between devices  172 us (27%)
  matrix products  70.6 us (11%)
  local copies, waits for them, and re-layouts  54.7 us (9%)
  other arithmetic  30.1 us (5%)
  between operations  14.3 us (2%)
    ppermute x48, starting transfers between devices, passed_along(): return lax.ppermute(x, axis, pairs)  172 us
    reduce_scatter x1, waiting for transfers between devices, body(): lax.psum_scatter(projected.astype(jnp.bfloat16), 'tp', scatter_dimension=...  143 us
    ppermute x48, waiting for transfers between devices, passed_along(): return lax.ppermute(x, axis, pairs)  91.2 us
    all_gather x1, waiting for transfers between devices, body(): gathered = lax.all_gather(residual, 'tp', axis=1, tiled=True)  52.2 us
    scatter x17, local copies, waits for them, and re-layouts, absorb(): cache_rows = cache_rows.at[target].set(incoming[0], mode='drop')  50.2 us
    dot_general x17, matrix products, attend_block(): jnp.einsum('hqk,khd->qhd', weights.astype(jnp.bfloat16), key_value[:, :,...  48.4 us
    reduce_sum x17, other arithmetic, attend_block(): norm_sum = norm_sum * shrink + jnp.sum(weights, axis=2)  15.5 us
    dot_general x17, matrix products, attend_block(): jnp.einsum('qhd,khd->hqk', queries, key_value[:, :, 0, :], preferred_elem...  15.4 us
  transfers between devices with their start and end apart: 50, of which 18 were waited for; matrix products, arithmetic and copies ran while one was open for 1% of the time, Pallas kernels for 0%

commit v1 on v0

--- a/solution.py
+++ b/solution.py
@@ -43,7 +43,8 @@
 ):
     row_count = residual.shape[0]
     local_heads = query_weight.shape[1] // HD
-    gathered = lax.all_gather(residual, "tp", axis=1, tiled=True)
+    outgoing = jnp.stack([residual] * lax.axis_size("tp"))
+    gathered = jnp.concatenate(lax.all_to_all(outgoing, "tp", 0, 0), axis=1)
     widened = gathered.astype(jnp.float32)
     mean_sq = jnp.mean(widened * widened, axis=1, keepdims=True)
     normed = (widened * lax.rsqrt(mean_sq + EPS) * norm_gain[None, :]).astype(jnp.bfloat16)

time: 634 us -> 636 us (level)
  waiting for transfers between devices: 287 us -> 274 us
  local copies, waits for them, and re-layouts: 54.7 us -> 66 us
  starting transfers between devices: 172 us -> 181 us
    all_gather x1 -> x0, waiting for transfers between devices: 52.2 us -> none  [body(): gathered = lax.all_gather(residual, 'tp', axis=1, tiled=True)]
    all_to_all x0 -> x1, waiting for transfers between devices: none -> 41.1 us  [body(): gathered = jnp.concatenate(lax.all_to_all(outgoing, 'tp', 0, 0), axis=1)]
    all_to_all x0 -> x1, starting transfers between devices: none -> 6.43 us  [body(): gathered = jnp.concatenate(lax.all_to_all(outgoing, 'tp', 0, 0), axis=1)]
  transfers between devices with their start and end apart: 50 -> 50, of which waited for: 18 -> 18; matrix products, arithmetic and copies ran while one was open for 1% -> 2% of each run, Pallas kernels for 0% -> 0%
where the time goes in v1:
time: 636 us; the launch traced here: 633 us
  waiting for transfers between devices  274 us (43%)
  starting transfers between devices  181 us (28%)
  matrix products  68 us (11%)
  local copies, waits for them, and re-layouts  66 us (10%)
  other arithmetic  27.6 us (4%)
  between operations  14.3 us (2%)
    ppermute x48, starting transfers between devices, passed_along(): return lax.ppermute(x, axis, pairs)  174 us
    reduce_scatter x1, waiting for transfers between devices, body(): lax.psum_scatter(projected.astype(jnp.bfloat16), 'tp', scatter_dimension=...  142 us
    ppermute x48, waiting for transfers between devices, passed_along(): return lax.ppermute(x, axis, pairs)  91.2 us
    scatter x17, local copies, waits for them, and re-layouts, absorb(): cache_rows = cache_rows.at[target].set(incoming[0], mode='drop')  50.2 us
    dot_general x17, matrix products, attend_block(): jnp.einsum('hqk,khd->qhd', weights.astype(jnp.bfloat16), key_value[:, :,...  48.4 us
    all_to_all x1, waiting for transfers between devices, body(): gathered = jnp.concatenate(lax.all_to_all(outgoing, 'tp', 0, 0), axis=1)  41.1 us
    reduce_sum x17, other arithmetic, attend_block(): norm_sum = norm_sum * shrink + jnp.sum(weights, axis=2)  15.5 us
    dot_general x17, matrix products, attend_block(): jnp.einsum('qhd,khd->hqk', queries, key_value[:, :, 0, :], preferred_elem...  15.4 us
  transfers between devices with their start and end apart: 50, of which 18 were waited for; matrix products, arithmetic and copies ran while one was open for 2% of the time, Pallas kernels for 0%

profile of v1, /device:TPU:1, one launch (start us, length us, event | category | flops | bytes accessed | tf_op | source)
XLA Modules:
  0.0 633.0 jit_solution(5073541296367181563)
XLA Ops:
  9.9 6.4 %all-to-all-start = ((bf16[4,512,512]{2,1,0:T(8,128)(2,1)}), bf16[4,512,512]{2,1,0:T(8,128)(2,1)}, u32[]{:S(2)}, u32[]{:S(2)}) async-start(bf16[4,512,512]{2,1,0:T(8,128)(2,1)} %stack.2), calls=%async_computation | async-start | bytes 4194304 | tf_op jit(solution)/shard_map/all_to_all | solution.py:47
  23.1 41.1 %all-to-all-done = bf16[4,512,512]{2,1,0:T(8,128)(2,1)} async-done(((bf16[4,512,512]{2,1,0:T(8,128)(2,1)}), bf16[4,512,512]{2,1,0:T(8,128)(2,1)}, u32[]{:S(2)}, u32[]{:S(2)}) %all-to-all-start) | async-done | bytes 2097184 | tf_op jit(solution)/shard_map/all_to_all | solution.py:47
  78.3 400.6 %while.27 = (s32[]{:T(128)}, bf16[512,512]{0,1:T(8,128)(2,1)S(1)}, s32[512]{0:T(512)S(1)}, s32[512]{0:T(512)S(1)}, f32[4,512]{1,0:T(4,128)S(1)}, /*index=5*/f32[...) while((s32[]{:T(128)}, bf16[512,512]{0,1:T(8,128)(2,1)S(1)}, ...), condition=%wide.region_8.9_spmd.clone.clone, body=%wide.region_4.8_spmd.clone.clone.sunk | while | flops 281293824 | bytes 21409060 | solution.py:135
  78.3 4.4 collective-permute-start.2
  88.5 5.7 collective-permute-done
  102.3 4.4 collective-permute-start.2
  112.2 5.7 collective-permute-done
  125.9 4.4 collective-permute-start.2
  136.2 5.7 collective-permute-done
  149.9 4.4 collective-permute-start.2
  157.4 4.4 collective-permute-start
  162.2 5.7 collective-permute-done
  176.0 4.4 collective-permute-start.2
  182.3 4.0 collective-permute-start
  186.7 5.7 collective-permute-done
  200.5 4.4 collective-permute-start.2
  211.2 5.7 collective-permute-done
  224.9 4.4 collective-permute-start.2
  235.7 5.7 collective-permute-done
  249.4 4.4 collective-permute-start.2
  255.8 4.0 collective-permute-start
  260.2 5.7 collective-permute-done
  273.9 4.4 collective-permute-start.2
  280.2 4.0 collective-permute-start
  284.7 5.7 collective-permute-done
  298.4 4.4 collective-permute-start.2
  304.7 4.0 collective-permute-start
  309.2 5.7 collective-permute-done
  322.9 4.4 collective-permute-start.2
  329.2 4.0 collective-permute-start
  333.7 5.7 collective-permute-done
  347.4 4.4 collective-permute-start.2
  353.7 4.0 collective-permute-start
  358.2 5.7 collective-permute-done
  371.9 4.4 collective-permute-start.2
  378.2 4.0 collective-permute-start
  382.6 5.7 collective-permute-done
  396.4 4.4 collective-permute-start.2
  402.7 4.0 collective-permute-start
  407.1 5.7 collective-permute-done
  420.9 4.4 collective-permute-start.2
  428.4 4.4 collective-permute-start
  433.2 5.7 collective-permute-done
  446.9 4.4 collective-permute-start.2
  451.3 9.0 %collective-permute-start.1 = (s32[512]{0:T(512)S(1)}, s32[512]{0:T(512)S(1)}, u32[]{:S(2)}, u32[]{:S(2)}) collective-permute-start(s32[512]{0:T(512)S(1)} %get-tuple-element.427), channel_id=1, source_target_pairs={{0,4},{4,8},{8,12},{12,16},{16,20},{20,24},{24,28},{28,32},{32,36}... | collective-permute-start | bytes 6152 | tf_op jit(solution)/shard_map/while/body/eval_jaxpr/ppermute | solution.py:16
  460.3 4.4 collective-permute-start
  465.1 5.7 collective-permute-done
  482.5 141.7 %reduce-scatter.2.cloned.1.call-done = bf16[512,512]{1,0:T(8,128)(2,1)} async-done(((bf16[512,2048]{1,0:T(8,128)(2,1)}), bf16[512,512]{1,0:T(8,128)(2,1)}) %reduce-scatter.2.cloned.1.call-update) | async-done | bytes 524304 | tf_op jit(solution)/shard_map/reduce_scatter | solution.py:143
  (356 shorter events, 211.3 us)
Async XLA Ops:
  9.9 54.3 %all-to-all-start = ((bf16[4,512,512]{2,1,0:T(8,128)(2,1)}), bf16[4,512,512]{2,1,0:T(8,128)(2,1)}, u32[]{:S(2)}, u32[]{:S(2)}) async-start(bf16[4,512,512]{2,1,0:T(8,128)(2,1)} %stack.2), calls=%async_computation | async-start | bytes 4194304 | tf_op jit(solution)/shard_map/all_to_all | solution.py:47
  16.3 607.9 %reduce-scatter.2.cloned.1.call-start = ((), (), s32[]{:S(2)}) async-start(), calls=%async_computation.2 | async-start | bytes 2621440 | tf_op jit(solution)/shard_map/reduce_scatter | solution.py:143
  78.3 9.9 %collective-permute-start.2 = (s32[512]{0:T(512)S(1)}, s32[512]{0:T(512)S(1)}, u32[]{:S(2)}, u32[]{:S(2)}) collective-permute-start(s32[512]{0:T(512)S(1)} %get-tuple-element.428), channel_id=1, source_target_pairs={{0,4},{4,8},{8,12},{12,16},{16,20},{20,24},{24,28},{28,32},{32,36}... | collective-permute-start | bytes 6152 | tf_op jit(solution)/shard_map/while/body/eval_jaxpr/ppermute | solution.py:16
  82.7 5.5 collective-permute-start.1
  84.6 9.6 %collective-permute-start = (bf16[512,512]{0,1:T(8,128)(2,1)S(1)}, bf16[512,512]{0,1:T(8,128)(2,1)S(1)}, u32[]{:S(2)}, u32[]{:S(2)}) collective-permute-start(bf16[512,512]{0,1:T(8,128)(2,1)S(1)} %get-tuple-element.426), channel_id=1, source_target_pairs={{0,4},{4,8},{8,12},{12,16},{16,20},{20,24},{24,28},{28,32},{32,36}... | collective-permute-start | bytes 1572872 | tf_op jit(solution)/shard_map/while/body/eval_jaxpr/ppermute | solution.py:16
  102.3 9.6 %collective-permute-start.2 = (s32[512]{0:T(512)S(1)}, s32[512]{0:T(512)S(1)}, u32[]{:S(2)}, u32[]{:S(2)}) collective-permute-start(s32[512]{0:T(512)S(1)} %get-tuple-element.428), channel_id=1, source_target_pairs={{0,4},{4,8},{8,12},{12,16},{16,20},{20,24},{24,28},{28,32},{32,36}... | collective-permute-start | bytes 6152 | tf_op jit(solution)/shard_map/while/body/eval_jaxpr/ppermute | solution.py:16
  108.6 9.3 %collective-permute-start = (bf16[512,512]{0,1:T(8,128)(2,1)S(1)}, bf16[512,512]{0,1:T(8,128)(2,1)S(1)}, u32[]{:S(2)}, u32[]{:S(2)}) collective-permute-start(bf16[512,512]{0,1:T(8,128)(2,1)S(1)} %get-tuple-element.426), channel_id=1, source_target_pairs={{0,4},{4,8},{8,12},{12,16},{16,20},{20,24},{24,28},{28,32},{32,36}... | collective-permute-start | bytes 1572872 | tf_op jit(solution)/shard_map/while/body/eval_jaxpr/ppermute | solution.py:16
  125.9 9.9 %collective-permute-start.2 = (s32[512]{0:T(512)S(1)}, s32[512]{0:T(512)S(1)}, u32[]{:S(2)}, u32[]{:S(2)}) collective-permute-start(s32[512]{0:T(512)S(1)} %get-tuple-element.428), channel_id=1, source_target_pairs={{0,4},{4,8},{8,12},{12,16},{16,20},{20,24},{24,28},{28,32},{32,36}... | collective-permute-start | bytes 6152 | tf_op jit(solution)/shard_map/while/body/eval_jaxpr/ppermute | solution.py:16
  132.3 9.6 %collective-permute-start = (bf16[512,512]{0,1:T(8,128)(2,1)S(1)}, bf16[512,512]{0,1:T(8,128)(2,1)S(1)}, u32[]{:S(2)}, u32[]{:S(2)}) collective-permute-start(bf16[512,512]{0,1:T(8,128)(2,1)S(1)} %get-tuple-element.426), channel_id=1, source_target_pairs={{0,4},{4,8},{8,12},{12,16},{16,20},{20,24},{24,28},{28,32},{32,36}... | collective-permute-start | bytes 1572872 | tf_op jit(solution)/shard_map/while/body/eval_jaxpr/ppermute | solution.py:16
  149.9 12.0 %collective-permute-start.2 = (s32[512]{0:T(512)S(1)}, s32[512]{0:T(512)S(1)}, u32[]{:S(2)}, u32[]{:S(2)}) collective-permute-start(s32[512]{0:T(512)S(1)} %get-tuple-element.428), channel_id=1, source_target_pairs={{0,4},{4,8},{8,12},{12,16},{16,20},{20,24},{24,28},{28,32},{32,36}... | collective-permute-start | bytes 6152 | tf_op jit(solution)/shard_map/while/body/eval_jaxpr/ppermute | solution.py:16
  154.3 7.6 %collective-permute-start.1 = (s32[512]{0:T(512)S(1)}, s32[512]{0:T(512)S(1)}, u32[]{:S(2)}, u32[]{:S(2)}) collective-permute-start(s32[512]{0:T(512)S(1)} %get-tuple-element.427), channel_id=1, source_target_pairs={{0,4},{4,8},{8,12},{12,16},{16,20},{20,24},{24,28},{28,32},{32,36}... | collective-permute-start | bytes 6152 | tf_op jit(solution)/shard_map/while/body/eval_jaxpr/ppermute | solution.py:16
  157.4 10.5 %collective-permute-start = (bf16[512,512]{0,1:T(8,128)(2,1)S(1)}, bf16[512,512]{0,1:T(8,128)(2,1)S(1)}, u32[]{:S(2)}, u32[]{:S(2)}) collective-permute-start(bf16[512,512]{0,1:T(8,128)(2,1)S(1)} %get-tuple-element.426), channel_id=1, source_target_pairs={{0,4},{4,8},{8,12},{12,16},{16,20},{20,24},{24,28},{28,32},{32,36}... | collective-permute-start | bytes 1572872 | tf_op jit(solution)/shard_map/while/body/eval_jaxpr/ppermute | solution.py:16
  176.0 10.4 %collective-permute-start.2 = (s32[512]{0:T(512)S(1)}, s32[512]{0:T(512)S(1)}, u32[]{:S(2)}, u32[]{:S(2)}) collective-permute-start(s32[512]{0:T(512)S(1)} %get-tuple-element.428), channel_id=1, source_target_pairs={{0,4},{4,8},{8,12},{12,16},{16,20},{20,24},{24,28},{28,32},{32,36}... | collective-permute-start | bytes 6152 | tf_op jit(solution)/shard_map/while/body/eval_jaxpr/ppermute | solution.py:16
  180.4 6.0 collective-permute-start.1
  182.3 10.1 %collective-permute-start = (bf16[512,512]{0,1:T(8,128)(2,1)S(1)}, bf16[512,512]{0,1:T(8,128)(2,1)S(1)}, u32[]{:S(2)}, u32[]{:S(2)}) collective-permute-start(bf16[512,512]{0,1:T(8,128)(2,1)S(1)} %get-tuple-element.426), channel_id=1, source_target_pairs={{0,4},{4,8},{8,12},{12,16},{16,20},{20,24},{24,28},{28,32},{32,36}... | collective-permute-start | bytes 1572872 | tf_op jit(solution)/shard_map/while/body/eval_jaxpr/ppermute | solution.py:16
  200.5 10.4 %collective-permute-start.2 = (s32[512]{0:T(512)S(1)}, s32[512]{0:T(512)S(1)}, u32[]{:S(2)}, u32[]{:S(2)}) collective-permute-start(s32[512]{0:T(512)S(1)} %get-tuple-element.428), channel_id=1, source_target_pairs={{0,4},{4,8},{8,12},{12,16},{16,20},{20,24},{24,28},{28,32},{32,36}... | collective-permute-start | bytes 6152 | tf_op jit(solution)/shard_map/while/body/eval_jaxpr/ppermute | solution.py:16
  204.8 6.0 collective-permute-start.1
  206.8 10.1 %collective-permute-start = (bf16[512,512]{0,1:T(8,128)(2,1)S(1)}, bf16[512,512]{0,1:T(8,128)(2,1)S(1)}, u32[]{:S(2)}, u32[]{:S(2)}) collective-permute-start(bf16[512,512]{0,1:T(8,128)(2,1)S(1)} %get-tuple-element.426), channel_id=1, source_target_pairs={{0,4},{4,8},{8,12},{12,16},{16,20},{20,24},{24,28},{28,32},{32,36}... | collective-permute-start | bytes 1572872 | tf_op jit(solution)/shard_map/while/body/eval_jaxpr/ppermute | solution.py:16
  224.9 10.4 %collective-permute-start.2 = (s32[512]{0:T(512)S(1)}, s32[512]{0:T(512)S(1)}, u32[]{:S(2)}, u32[]{:S(2)}) collective-permute-start(s32[512]{0:T(512)S(1)} %get-tuple-element.428), channel_id=1, source_target_pairs={{0,4},{4,8},{8,12},{12,16},{16,20},{20,24},{24,28},{28,32},{32,36}... | collective-permute-start | bytes 6152 | tf_op jit(solution)/shard_map/while/body/eval_jaxpr/ppermute | solution.py:16
  229.3 6.0 collective-permute-start.1
  231.3 10.1 %collective-permute-start = (bf16[512,512]{0,1:T(8,128)(2,1)S(1)}, bf16[512,512]{0,1:T(8,128)(2,1)S(1)}, u32[]{:S(2)}, u32[]{:S(2)}) collective-permute-start(bf16[512,512]{0,1:T(8,128)(2,1)S(1)} %get-tuple-element.426), channel_id=1, source_target_pairs={{0,4},{4,8},{8,12},{12,16},{16,20},{20,24},{24,28},{28,32},{32,36}... | collective-permute-start | bytes 1572872 | tf_op jit(solution)/shard_map/while/body/eval_jaxpr/ppermute | solution.py:16
  249.4 10.4 %collective-permute-start.2 = (s32[512]{0:T(512)S(1)}, s32[512]{0:T(512)S(1)}, u32[]{:S(2)}, u32[]{:S(2)}) collective-permute-start(s32[512]{0:T(512)S(1)} %get-tuple-element.428), channel_id=1, source_target_pairs={{0,4},{4,8},{8,12},{12,16},{16,20},{20,24},{24,28},{28,32},{32,36}... | collective-permute-start | bytes 6152 | tf_op jit(solution)/shard_map/while/body/eval_jaxpr/ppermute | solution.py:16
  253.8 6.0 collective-permute-start.1
  255.8 10.1 %collective-permute-start = (bf16[512,512]{0,1:T(8,128)(2,1)S(1)}, bf16[512,512]{0,1:T(8,128)(2,1)S(1)}, u32[]{:S(2)}, u32[]{:S(2)}) collective-permute-start(bf16[512,512]{0,1:T(8,128)(2,1)S(1)} %get-tuple-element.426), channel_id=1, source_target_pairs={{0,4},{4,8},{8,12},{12,16},{16,20},{20,24},{24,28},{28,32},{32,36}... | collective-permute-start | bytes 1572872 | tf_op jit(solution)/shard_map/while/body/eval_jaxpr/ppermute | solution.py:16
  273.9 10.4 %collective-permute-start.2 = (s32[512]{0:T(512)S(1)}, s32[512]{0:T(512)S(1)}, u32[]{:S(2)}, u32[]{:S(2)}) collective-permute-start(s32[512]{0:T(512)S(1)} %get-tuple-element.428), channel_id=1, source_target_pairs={{0,4},{4,8},{8,12},{12,16},{16,20},{20,24},{24,28},{28,32},{32,36}... | collective-permute-start | bytes 6152 | tf_op jit(solution)/shard_map/while/body/eval_jaxpr/ppermute | solution.py:16
  278.3 6.0 collective-permute-start.1
  280.2 10.1 %collective-permute-start = (bf16[512,512]{0,1:T(8,128)(2,1)S(1)}, bf16[512,512]{0,1:T(8,128)(2,1)S(1)}, u32[]{:S(2)}, u32[]{:S(2)}) collective-permute-start(bf16[512,512]{0,1:T(8,128)(2,1)S(1)} %get-tuple-element.426), channel_id=1, source_target_pairs={{0,4},{4,8},{8,12},{12,16},{16,20},{20,24},{24,28},{28,32},{32,36}... | collective-permute-start | bytes 1572872 | tf_op jit(solution)/shard_map/while/body/eval_jaxpr/ppermute | solution.py:16
  298.4 10.4 %collective-permute-start.2 = (s32[512]{0:T(512)S(1)}, s32[512]{0:T(512)S(1)}, u32[]{:S(2)}, u32[]{:S(2)}) collective-permute-start(s32[512]{0:T(512)S(1)} %get-tuple-element.428), channel_id=1, source_target_pairs={{0,4},{4,8},{8,12},{12,16},{16,20},{20,24},{24,28},{28,32},{32,36}... | collective-permute-start | bytes 6152 | tf_op jit(solution)/shard_map/while/body/eval_jaxpr/ppermute | solution.py:16
  302.8 6.0 collective-permute-start.1
  304.7 10.1 %collective-permute-start = (bf16[512,512]{0,1:T(8,128)(2,1)S(1)}, bf16[512,512]{0,1:T(8,128)(2,1)S(1)}, u32[]{:S(2)}, u32[]{:S(2)}) collective-permute-start(bf16[512,512]{0,1:T(8,128)(2,1)S(1)} %get-tuple-element.426), channel_id=1, source_target_pairs={{0,4},{4,8},{8,12},{12,16},{16,20},{20,24},{24,28},{28,32},{32,36}... | collective-permute-start | bytes 1572872 | tf_op jit(solution)/shard_map/while/body/eval_jaxpr/ppermute | solution.py:16
  322.9 10.4 %collective-permute-start.2 = (s32[512]{0:T(512)S(1)}, s32[512]{0:T(512)S(1)}, u32[]{:S(2)}, u32[]{:S(2)}) collective-permute-start(s32[512]{0:T(512)S(1)} %get-tuple-element.428), channel_id=1, source_target_pairs={{0,4},{4,8},{8,12},{12,16},{16,20},{20,24},{24,28},{28,32},{32,36}... | collective-permute-start | bytes 6152 | tf_op jit(solution)/shard_map/while/body/eval_jaxpr/ppermute | solution.py:16
  327.3 6.0 collective-permute-start.1
  329.2 10.1 %collective-permute-start = (bf16[512,512]{0,1:T(8,128)(2,1)S(1)}, bf16[512,512]{0,1:T(8,128)(2,1)S(1)}, u32[]{:S(2)}, u32[]{:S(2)}) collective-permute-start(bf16[512,512]{0,1:T(8,128)(2,1)S(1)} %get-tuple-element.426), channel_id=1, source_target_pairs={{0,4},{4,8},{8,12},{12,16},{16,20},{20,24},{24,28},{28,32},{32,36}... | collective-permute-start | bytes 1572872 | tf_op jit(solution)/shard_map/while/body/eval_jaxpr/ppermute | solution.py:16
  347.4 10.4 %collective-permute-start.2 = (s32[512]{0:T(512)S(1)}, s32[512]{0:T(512)S(1)}, u32[]{:S(2)}, u32[]{:S(2)}) collective-permute-start(s32[512]{0:T(512)S(1)} %get-tuple-element.428), channel_id=1, source_target_pairs={{0,4},{4,8},{8,12},{12,16},{16,20},{20,24},{24,28},{28,32},{32,36}... | collective-permute-start | bytes 6152 | tf_op jit(solution)/shard_map/while/body/eval_jaxpr/ppermute | solution.py:16
  351.8 6.0 collective-permute-start.1
  353.7 10.1 %collective-permute-start = (bf16[512,512]{0,1:T(8,128)(2,1)S(1)}, bf16[512,512]{0,1:T(8,128)(2,1)S(1)}, u32[]{:S(2)}, u32[]{:S(2)}) collective-permute-start(bf16[512,512]{0,1:T(8,128)(2,1)S(1)} %get-tuple-element.426), channel_id=1, source_target_pairs={{0,4},{4,8},{8,12},{12,16},{16,20},{20,24},{24,28},{28,32},{32,36}... | collective-permute-start | bytes 1572872 | tf_op jit(solution)/shard_map/while/body/eval_jaxpr/ppermute | solution.py:16
  371.9 10.4 %collective-permute-start.2 = (s32[512]{0:T(512)S(1)}, s32[512]{0:T(512)S(1)}, u32[]{:S(2)}, u32[]{:S(2)}) collective-permute-start(s32[512]{0:T(512)S(1)} %get-tuple-element.428), channel_id=1, source_target_pairs={{0,4},{4,8},{8,12},{12,16},{16,20},{20,24},{24,28},{28,32},{32,36}... | collective-permute-start | bytes 6152 | tf_op jit(solution)/shard_map/while/body/eval_jaxpr/ppermute | solution.py:16
  376.3 6.0 collective-permute-start.1
  378.2 10.1 %collective-permute-start = (bf16[512,512]{0,1:T(8,128)(2,1)S(1)}, bf16[512,512]{0,1:T(8,128)(2,1)S(1)}, u32[]{:S(2)}, u32[]{:S(2)}) collective-permute-start(bf16[512,512]{0,1:T(8,128)(2,1)S(1)} %get-tuple-element.426), channel_id=1, source_target_pairs={{0,4},{4,8},{8,12},{12,16},{16,20},{20,24},{24,28},{28,32},{32,36}... | collective-permute-start | bytes 1572872 | tf_op jit(solution)/shard_map/while/body/eval_jaxpr/ppermute | solution.py:16
  396.4 10.4 %collective-permute-start.2 = (s32[512]{0:T(512)S(1)}, s32[512]{0:T(512)S(1)}, u32[]{:S(2)}, u32[]{:S(2)}) collective-permute-start(s32[512]{0:T(512)S(1)} %get-tuple-element.428), channel_id=1, source_target_pairs={{0,4},{4,8},{8,12},{12,16},{16,20},{20,24},{24,28},{28,32},{32,36}... | collective-permute-start | bytes 6152 | tf_op jit(solution)/shard_map/while/body/eval_jaxpr/ppermute | solution.py:16
  400.8 6.0 collective-permute-start.1
  402.7 10.1 %collective-permute-start = (bf16[512,512]{0,1:T(8,128)(2,1)S(1)}, bf16[512,512]{0,1:T(8,128)(2,1)S(1)}, u32[]{:S(2)}, u32[]{:S(2)}) collective-permute-start(bf16[512,512]{0,1:T(8,128)(2,1)S(1)} %get-tuple-element.426), channel_id=1, source_target_pairs={{0,4},{4,8},{8,12},{12,16},{16,20},{20,24},{24,28},{28,32},{32,36}... | collective-permute-start | bytes 1572872 | tf_op jit(solution)/shard_map/while/body/eval_jaxpr/ppermute | solution.py:16
  420.9 12.0 %collective-permute-start.2 = (s32[512]{0:T(512)S(1)}, s32[512]{0:T(512)S(1)}, u32[]{:S(2)}, u32[]{:S(2)}) collective-permute-start(s32[512]{0:T(512)S(1)} %get-tuple-element.428), channel_id=1, source_target_pairs={{0,4},{4,8},{8,12},{12,16},{16,20},{20,24},{24,28},{28,32},{32,36}... | collective-permute-start | bytes 6152 | tf_op jit(solution)/shard_map/while/body/eval_jaxpr/ppermute | solution.py:16
  425.2 7.6 %collective-permute-start.1 = (s32[512]{0:T(512)S(1)}, s32[512]{0:T(512)S(1)}, u32[]{:S(2)}, u32[]{:S(2)}) collective-permute-start(s32[512]{0:T(512)S(1)} %get-tuple-element.427), channel_id=1, source_target_pairs={{0,4},{4,8},{8,12},{12,16},{16,20},{20,24},{24,28},{28,32},{32,36}... | collective-permute-start | bytes 6152 | tf_op jit(solution)/shard_map/while/body/eval_jaxpr/ppermute | solution.py:16
  428.4 10.5 %collective-permute-start = (bf16[512,512]{0,1:T(8,128)(2,1)S(1)}, bf16[512,512]{0,1:T(8,128)(2,1)S(1)}, u32[]{:S(2)}, u32[]{:S(2)}) collective-permute-start(bf16[512,512]{0,1:T(8,128)(2,1)S(1)} %get-tuple-element.426), channel_id=1, source_target_pairs={{0,4},{4,8},{8,12},{12,16},{16,20},{20,24},{24,28},{28,32},{32,36}... | collective-permute-start | bytes 1572872 | tf_op jit(solution)/shard_map/while/body/eval_jaxpr/ppermute | solution.py:16
  446.9 17.8 %collective-permute-start.2 = (s32[512]{0:T(512)S(1)}, s32[512]{0:T(512)S(1)}, u32[]{:S(2)}, u32[]{:S(2)}) collective-permute-start(s32[512]{0:T(512)S(1)} %get-tuple-element.428), channel_id=1, source_target_pairs={{0,4},{4,8},{8,12},{12,16},{16,20},{20,24},{24,28},{28,32},{32,36}... | collective-permute-start | bytes 6152 | tf_op jit(solution)/shard_map/while/body/eval_jaxpr/ppermute | solution.py:16
  451.3 13.4 %collective-permute-start.1 = (s32[512]{0:T(512)S(1)}, s32[512]{0:T(512)S(1)}, u32[]{:S(2)}, u32[]{:S(2)}) collective-permute-start(s32[512]{0:T(512)S(1)} %get-tuple-element.427), channel_id=1, source_target_pairs={{0,4},{4,8},{8,12},{12,16},{16,20},{20,24},{24,28},{28,32},{32,36}... | collective-permute-start | bytes 6152 | tf_op jit(solution)/shard_map/while/body/eval_jaxpr/ppermute | solution.py:16
  460.3 10.5 %collective-permute-start = (bf16[512,512]{0,1:T(8,128)(2,1)S(1)}, bf16[512,512]{0,1:T(8,128)(2,1)S(1)}, u32[]{:S(2)}, u32[]{:S(2)}) collective-permute-start(bf16[512,512]{0,1:T(8,128)(2,1)S(1)} %get-tuple-element.426), channel_id=1, source_target_pairs={{0,4},{4,8},{8,12},{12,16},{16,20},{20,24},{24,28},{28,32},{32,36}... | collective-permute-start | bytes 1572872 | tf_op jit(solution)/shard_map/while/body/eval_jaxpr/ppermute | solution.py:16
  (15 other events, 826.5 us)
Sparse Core Ops, SparseCore 0:
  482.6 141.5 reduce-scatter.1
